TPU v7x, 256 devices: a whole 4x4x8 slice. The times are simulated.
256 devices in a mesh: tm: 64 (over z, y, core), ingest: 4 (over x).
Axes of the slice: x: 4, y: 4, z: 8, core: 2. Of those that a mesh axis runs over, the one named last changes fastest.
Arguments:
- trans: float32 [512, 384, 384], P('tm')
- gain: float32 [512, 384, 192], P('tm', None, 'ingest'), may hold values from -0.0048828125 to 0.0048828125
- prior_mean: float32 [384], replicated, may hold values from -8 to 8
- obs_basis: bfloat16 [131072, 192], P(('tm', 'ingest')), may hold values from -6 to 6
- obs_value: float32 [131072], P(('tm', 'ingest')), may hold values from -6 to 6
- measurement_within_tile: int32 [131072], P(('tm', 'ingest')), may hold values from 0 to 7
- observed_row_count: int32 [256, 64], P(('tm', 'ingest')), may hold values from 1 to 8, as said below
Outputs:
- filtered: float32 [512, 384], P('tm')
Inputs may be any that keep to these rules, and one draw needn't show every extreme that they name: `observed_row_count`: rows of a group at positions from its count on are not live; every device's row of counts has one group of 8 live rows.
All inputs are finite; a program needn't handle non-finite values.
Results may differ from a plain program's by a relative error of at most 0.0023.
Values may be sent and summed in bfloat16 or wider, within the bound.
No kernel may reach another device: no remote copies, remote signals or barrier semaphores. Data moves between devices by JAX's collectives and lax.ppermute only.
A program may use at most 128 MiB of HBM per device.

v0:
```python
import jax
import jax.numpy as jnp
from jax import lax
from jax.sharding import PartitionSpec as P


def passed_along(block, axis, distance):
    devices = range(lax.axis_size(axis))
    route = [(i - distance, i) for i in devices if i - distance in devices]
    return lax.ppermute(block, axis, route)


def on_device(
    trans, gain, prior_mean, obs_basis, obs_value, measurement_within_tile, observed_row_count
):
    exact = lax.Precision.HIGHEST
    tm_count = lax.axis_size("tm")
    in_count = lax.axis_size("ingest")
    steps_here = trans.shape[0]
    state_width = trans.shape[1]
    basis_count = obs_basis.shape[1]
    piece_width = basis_count // in_count
    group_rows = obs_basis.shape[0] // tm_count
    weighted = (obs_basis.astype(jnp.float32) * obs_value[:, None]).astype(jnp.bfloat16)
    pieces = weighted.reshape(tm_count, group_rows, in_count, piece_width)
    pieces = pieces.transpose(0, 2, 1, 3).reshape(tm_count * in_count, group_rows * piece_width)
    is_valid = lax.broadcasted_iota(
        jnp.int32, (tm_count, group_rows), 1
    ) < observed_row_count.reshape(tm_count, 1)
    marked = jnp.where(is_valid, measurement_within_tile.reshape(tm_count, group_rows), -1)
    marks = jnp.broadcast_to(
        marked.astype(jnp.bfloat16)[:, None, :], (tm_count, in_count, group_rows)
    ).reshape(tm_count * in_count, group_rows)
    sent = jnp.concatenate([pieces, marks], axis=1)
    got = lax.all_to_all(sent, ("tm", "ingest"), split_axis=0, concat_axis=0, tiled=True)
    got_rows = got[:, : group_rows * piece_width].reshape(-1, piece_width)
    got_marks = got[:, group_rows * piece_width :].reshape(-1).astype(jnp.int32)
    step_ids = lax.broadcasted_iota(jnp.int32, (1, steps_here), 1)
    onehot = (got_marks[:, None] == step_ids).astype(jnp.bfloat16)
    drive_piece = jnp.einsum("rl,rq->lq", onehot, got_rows, preferred_element_type=jnp.float32)
    partial_force = jnp.einsum("lsq,lq->ls", gain, drive_piece, precision=exact)
    forcing = lax.psum(partial_force, "ingest")

    def compose(prefix, step_map):
        prefix = jnp.dot(step_map, prefix, precision=exact)
        return (prefix, prefix)

    _, prefix_maps = lax.scan(compose, jnp.eye(state_width, dtype=jnp.float32), trans)

    def advance(offset, inputs):
        step_map, step_force = inputs
        offset = jnp.dot(step_map, offset, precision=exact) + step_force
        return (offset, offset)

    _, offsets = lax.scan(advance, jnp.zeros((state_width,), jnp.float32), (trans, forcing))
    tm_index = lax.axis_index("tm")
    is_first = tm_index == 0
    slab_map = prefix_maps[-1]
    acc_vec = jnp.where(
        is_first, jnp.dot(slab_map, prior_mean, precision=exact) + offsets[-1], offsets[-1]
    )
    acc_map = jnp.where(is_first, jnp.zeros_like(slab_map), slab_map)
    distance = 1
    while distance < tm_count:
        got_vec = passed_along(acc_vec, "tm", distance)
        last = distance * 2 >= tm_count
        if not last:
            got_map = passed_along(acc_map, "tm", distance)
        acc_vec = jnp.dot(acc_map, got_vec, precision=exact) + acc_vec
        if not last:
            acc_map = jnp.dot(acc_map, got_map, precision=exact)
        distance *= 2
    entering = jnp.where(is_first, prior_mean, passed_along(acc_vec, "tm", 1))
    filtered = jnp.einsum("lsq,q->ls", prefix_maps, entering, precision=exact) + offsets
    return filtered


def solution(mesh):
    return jax.shard_map(
        on_device,
        mesh=mesh,
        in_specs=(
            P("tm", None, None),
            P("tm", None, "ingest"),
            P(),
            P(("tm", "ingest"), None),
            P(("tm", "ingest")),
            P(("tm", "ingest")),
            P(("tm", "ingest"), None),
        ),
        out_specs=P("tm", None),
        check_vma=False,
    )
```

profile of v0, /device:TPU:128, one launch (start us, length us, event | category | flops | bytes accessed | tf_op | source)
XLA Modules:
  0.0 224.0 jit_solution(79529686420630875)
XLA Ops:
  0.1 25.7 %while.25 = (s32[]{:T(128)}, f32[384,384]{1,0:T(8,128)S(1)}, f32[8,384,384]{2,1,0:T(8,128)}, f32[8,384,384]{2,1,0:T(8,128)}, s32[]{:T(128)}) while((s32[]{:T(128)}, f32[384,384]{1,0:T(8,128)S(1)}, f32[8,384,384]{2,1,0:T(8,128)}, f32[8,384,384]{2,1,0:T(8,128)}, s32[]{:T(128)}) %tuple.41), condition=%wide.region_1.2_spmd, body=%wide.region_0.1_spmd.sunk | while | flops 679477248 | bytes 3540037 | solution.py:48
  0.2 3.2 %bitcast_dynamic-update-slice_fusion.2 = (f32[8,384,384]{2,1,0:T(8,128)}, f32[384,384]{1,0:T(8,128)S(1)}) fusion(f32[8,384,384]{2,1,0:T(8,128)} %get-tuple-element.182, s32[]{:T(128)S(6)} %copy.40, f32[384,384]{1,0:T(8,128)S(1)} %copy.47, f32[8,384,384]{2,1,0:T(8,128)} %get-tuple-element.188), kind=kOutput, calls=%fused_computation.clone.1 | convolution fusion | flops 679477248 | bytes 2360320 | tf_op jit(solution)/shard_map/while/body/eval_jaxpr/dot_general | solution.py:45
  3.4 3.1 %bitcast_dynamic-update-slice_fusion.2 = (f32[8,384,384]{2,1,0:T(8,128)}, f32[384,384]{1,0:T(8,128)S(1)}) fusion(f32[8,384,384]{2,1,0:T(8,128)} %get-tuple-element.182, s32[]{:T(128)S(6)} %copy.40, f32[384,384]{1,0:T(8,128)S(1)} %copy.47, f32[8,384,384]{2,1,0:T(8,128)} %get-tuple-element.188), kind=kOutput, calls=%fused_computation.clone.1 | convolution fusion | flops 679477248 | bytes 2360320 | tf_op jit(solution)/shard_map/while/body/eval_jaxpr/dot_general | solution.py:45
  6.6 3.2 %bitcast_dynamic-update-slice_fusion.2 = (f32[8,384,384]{2,1,0:T(8,128)}, f32[384,384]{1,0:T(8,128)S(1)}) fusion(f32[8,384,384]{2,1,0:T(8,128)} %get-tuple-element.182, s32[]{:T(128)S(6)} %copy.40, f32[384,384]{1,0:T(8,128)S(1)} %copy.47, f32[8,384,384]{2,1,0:T(8,128)} %get-tuple-element.188), kind=kOutput, calls=%fused_computation.clone.1 | convolution fusion | flops 679477248 | bytes 2360320 | tf_op jit(solution)/shard_map/while/body/eval_jaxpr/dot_general | solution.py:45
  9.8 3.2 %bitcast_dynamic-update-slice_fusion.2 = (f32[8,384,384]{2,1,0:T(8,128)}, f32[384,384]{1,0:T(8,128)S(1)}) fusion(f32[8,384,384]{2,1,0:T(8,128)} %get-tuple-element.182, s32[]{:T(128)S(6)} %copy.40, f32[384,384]{1,0:T(8,128)S(1)} %copy.47, f32[8,384,384]{2,1,0:T(8,128)} %get-tuple-element.188), kind=kOutput, calls=%fused_computation.clone.1 | convolution fusion | flops 679477248 | bytes 2360320 | tf_op jit(solution)/shard_map/while/body/eval_jaxpr/dot_general | solution.py:45
  13.0 3.2 %bitcast_dynamic-update-slice_fusion.2 = (f32[8,384,384]{2,1,0:T(8,128)}, f32[384,384]{1,0:T(8,128)S(1)}) fusion(f32[8,384,384]{2,1,0:T(8,128)} %get-tuple-element.182, s32[]{:T(128)S(6)} %copy.40, f32[384,384]{1,0:T(8,128)S(1)} %copy.47, f32[8,384,384]{2,1,0:T(8,128)} %get-tuple-element.188), kind=kOutput, calls=%fused_computation.clone.1 | convolution fusion | flops 679477248 | bytes 2360320 | tf_op jit(solution)/shard_map/while/body/eval_jaxpr/dot_general | solution.py:45
  16.2 3.1 %bitcast_dynamic-update-slice_fusion.2 = (f32[8,384,384]{2,1,0:T(8,128)}, f32[384,384]{1,0:T(8,128)S(1)}) fusion(f32[8,384,384]{2,1,0:T(8,128)} %get-tuple-element.182, s32[]{:T(128)S(6)} %copy.40, f32[384,384]{1,0:T(8,128)S(1)} %copy.47, f32[8,384,384]{2,1,0:T(8,128)} %get-tuple-element.188), kind=kOutput, calls=%fused_computation.clone.1 | convolution fusion | flops 679477248 | bytes 2360320 | tf_op jit(solution)/shard_map/while/body/eval_jaxpr/dot_general | solution.py:45
  19.4 3.1 %bitcast_dynamic-update-slice_fusion.2 = (f32[8,384,384]{2,1,0:T(8,128)}, f32[384,384]{1,0:T(8,128)S(1)}) fusion(f32[8,384,384]{2,1,0:T(8,128)} %get-tuple-element.182, s32[]{:T(128)S(6)} %copy.40, f32[384,384]{1,0:T(8,128)S(1)} %copy.47, f32[8,384,384]{2,1,0:T(8,128)} %get-tuple-element.188), kind=kOutput, calls=%fused_computation.clone.1 | convolution fusion | flops 679477248 | bytes 2360320 | tf_op jit(solution)/shard_map/while/body/eval_jaxpr/dot_general | solution.py:45
  22.6 3.1 %bitcast_dynamic-update-slice_fusion.2 = (f32[8,384,384]{2,1,0:T(8,128)}, f32[384,384]{1,0:T(8,128)S(1)}) fusion(f32[8,384,384]{2,1,0:T(8,128)} %get-tuple-element.182, s32[]{:T(128)S(6)} %copy.40, f32[384,384]{1,0:T(8,128)S(1)} %copy.47, f32[8,384,384]{2,1,0:T(8,128)} %get-tuple-element.188), kind=kOutput, calls=%fused_computation.clone.1 | convolution fusion | flops 679477248 | bytes 2360320 | tf_op jit(solution)/shard_map/while/body/eval_jaxpr/dot_general | solution.py:45
  26.9 1.9 collective-permute-start
  29.0 12.4 %collective-permute-done = f32[384,384]{1,0:T(8,128)S(1)} collective-permute-done((f32[384,384]{1,0:T(8,128)S(1)}, f32[384,384]{1,0:T(8,128)S(1)}, u32[]{:S(2)}, u32[]{:S(2)}) %collective-permute-start) | collective-permute-done | bytes 589856 | tf_op jit(solution)/shard_map/ppermute | solution.py:10
  42.7 1.9 collective-permute-start.1
  47.8 13.9 %all-to-all-start = ((bf16[256,2,196]{2,1,0:T(2,128)(2,1)}), bf16[256,2,196]{2,1,0:T(2,128)(2,1)S(1)}, u32[]{:S(2)}, u32[]{:S(2)}) async-start(bf16[256,2,196]{2,1,0:T(2,128)(2,1)} %reshape.87), calls=%async_computation | async-start | bytes 524288 | tf_op jit(solution)/shard_map/all_to_all | solution.py:35
  61.8 1.7 convolution_reduce_fusion.7
  63.5 8.7 %all-to-all-done = bf16[256,2,196]{2,1,0:T(2,128)(2,1)S(1)} async-done(((bf16[256,2,196]{2,1,0:T(2,128)(2,1)}), bf16[256,2,196]{2,1,0:T(2,128)(2,1)S(1)}, u32[]{:S(2)}, u32[]{:S(2)}) %all-to-all-start) | async-done | bytes 200736 | tf_op jit(solution)/shard_map/all_to_all | solution.py:35
  74.2 3.3 %collective-permute-start.2 = (f32[384,384]{1,0:T(8,128)S(1)}, f32[384,384]{1,0:T(8,128)S(1)}, u32[]{:S(2)}, u32[]{:S(2)}) collective-permute-start(f32[384,384]{1,0:T(8,128)S(1)} %fusion.13), channel_id=1, source_target_pairs={{0,16},{4,20},{8,24},{12,28},{16,32},{20,36},{24,40},{28,44},{32,4... | collective-permute-start | bytes 1769480 | tf_op jit(solution)/shard_map/ppermute | solution.py:10
  79.2 1.7 fusion.7
  81.4 15.5 %psum.7 = f32[8,384]{1,0:T(8,128)} all-reduce(f32[8,384]{1,0:T(8,128)S(1)} %bitcast.74), channel_id=1, replica_groups=mesh['tm'=64,'ingest'=4] {'ingest'}, use_global_device_ids=true, to_apply=%region_2.3 | all-reduce | flops 3072 | bytes 24576 | tf_op jit(solution)/shard_map/psum | solution.py:42
  98.2 2.6 %collective-permute-start.3 = (f32[384,384]{1,0:T(8,128)S(1)}, f32[384,384]{1,0:T(8,128)S(1)}, u32[]{:S(2)}, u32[]{:S(2)}) collective-permute-start(f32[384,384]{1,0:T(8,128)S(1)} %fusion.14), channel_id=1, source_target_pairs={{0,32},{4,36},{8,40},{12,44},{16,48},{20,52},{24,56},{28,60},{32,6... | collective-permute-start | bytes 1769480 | tf_op jit(solution)/shard_map/ppermute | solution.py:10
  100.7 30.5 %while.26 = (s32[]{:T(128)}, f32[384]{0:T(512)S(1)}, f32[8,384]{1,0:T(8,128)}, f32[8,384,384]{2,1,0:T(8,128)}, f32[8,384]{1,0:T(8,128)}, /*index=5*/s32[]{:T(128)}, s32[]{:T(128)}) while((s32[]{:T(128)}, f32[384]{0:T(512)S(1)}, f32[8,384]{1,0:T(8,128)}, f32[8,384,384]{2,1,0:T(8,128)}, f32[8,384]{1,0:T(8,128)}, ...), condition=%wide.region_4.5_spmd.clone, body=%wide.region_3.4_spmd.clone.sunk | while | flops 1770243 | bytes 612971 | solution.py:55
  100.8 1.7 convolution_reduce_fusion.9
  103.3 1.3 dynamic_update_slice.13
  104.6 1.7 convolution_reduce_fusion.9
  107.1 1.3 dynamic_update_slice.13
  108.4 1.7 convolution_reduce_fusion.9
  110.9 1.3 dynamic_update_slice.13
  112.2 1.7 convolution_reduce_fusion.9
  114.7 1.3 dynamic_update_slice.13
  116.0 1.7 convolution_reduce_fusion.9
  118.5 1.3 dynamic_update_slice.13
  119.8 1.7 convolution_reduce_fusion.9
  123.6 1.7 convolution_reduce_fusion.9
  127.5 1.7 convolution_reduce_fusion.9
  132.0 2.1 collective-permute-start.5
  134.1 6.1 %collective-permute-done.5 = f32[384]{0:T(512)S(1)} collective-permute-done((f32[384]{0:T(512)S(1)}, f32[384]{0:T(512)S(1)}, u32[]{:S(2)}, u32[]{:S(2)}) %collective-permute-start.5) | collective-permute-done | bytes 1568 | tf_op jit(solution)/shard_map/ppermute | solution.py:10
  141.5 2.9 %collective-permute-start.4 = (f32[384,384]{1,0:T(8,128)S(1)}, f32[384,384]{1,0:T(8,128)S(1)}, u32[]{:S(2)}, u32[]{:S(2)}) collective-permute-start(f32[384,384]{1,0:T(8,128)S(1)} %fusion.15), channel_id=1, source_target_pairs={{0,64},{4,68},{8,72},{12,76},{16,80},{20,84},{24,88},{28,92},{32,9... | collective-permute-start | bytes 1769480 | tf_op jit(solution)/shard_map/ppermute | solution.py:10
  145.1 1.9 collective-permute-start.6
  147.0 24.4 %collective-permute-done.6 = f32[384]{0:T(512)S(1)} collective-permute-done((f32[384]{0:T(512)S(1)}, f32[384]{0:T(512)S(1)}, u32[]{:S(2)}, u32[]{:S(2)}) %collective-permute-start.6) | collective-permute-done | bytes 1568 | tf_op jit(solution)/shard_map/ppermute | solution.py:10
  172.1 1.9 collective-permute-start.7
  174.0 7.2 %collective-permute-done.7 = f32[384]{0:T(512)S(1)} collective-permute-done((f32[384]{0:T(512)S(1)}, f32[384]{0:T(512)S(1)}, u32[]{:S(2)}, u32[]{:S(2)}) %collective-permute-start.7) | collective-permute-done | bytes 1568 | tf_op jit(solution)/shard_map/ppermute | solution.py:10
  181.8 1.9 collective-permute-start.8
  183.8 4.8 %collective-permute-done.8 = f32[384]{0:T(512)S(1)} collective-permute-done((f32[384]{0:T(512)S(1)}, f32[384]{0:T(512)S(1)}, u32[]{:S(2)}, u32[]{:S(2)}) %collective-permute-start.8) | collective-permute-done | bytes 1568 | tf_op jit(solution)/shard_map/ppermute | solution.py:10
  189.2 1.9 collective-permute-start.9
  191.1 5.7 %collective-permute-done.9 = f32[384]{0:T(512)S(1)} collective-permute-done((f32[384]{0:T(512)S(1)}, f32[384]{0:T(512)S(1)}, u32[]{:S(2)}, u32[]{:S(2)}) %collective-permute-start.9) | collective-permute-done | bytes 1568 | tf_op jit(solution)/shard_map/ppermute | solution.py:10
  198.8 8.1 %collective-permute-done.10 = f32[384]{0:T(512)S(1)} collective-permute-done((f32[384]{0:T(512)S(1)}, f32[384]{0:T(512)S(1)}, u32[]{:S(2)}, u32[]{:S(2)}) %collective-permute-start.10) | collective-permute-done | bytes 1568 | tf_op jit(solution)/shard_map/ppermute | solution.py:10
  208.8 1.9 collective-permute-start.11
  210.8 6.3 %collective-permute-done.11 = f32[384]{0:T(512)S(1)} collective-permute-done((f32[384]{0:T(512)S(1)}, f32[384]{0:T(512)S(1)}, u32[]{:S(2)}, u32[]{:S(2)}) %collective-permute-start.11) | collective-permute-done | bytes 1568 | tf_op jit(solution)/shard_map/ppermute | solution.py:10
  217.1 6.4 %fusion.18 = f32[1,8,384]{2,0,1:T(1,128)S(1)} fusion(f32[8,384,384]{2,1,0:T(8,128)} %get-tuple-element.54, f32[384,1,1]{0,1,2:T(1,128)S(1)} %reshape.75), kind=kOutput, calls=%fused_computation.42 | convolution fusion | flops 14155776 | bytes 4732416 | tf_op jit(solution)/shard_map/lsq,q->ls/dot_general | solution.py:74
  (126 shorter events, 30.7 us)
Async XLA Ops:
  0.0 80.9 %copy-start = (f32[8,384,48]{1,2,0:T(8,128)S(1)}, f32[8,384,48]{1,2,0:T(8,128)}, u32[]{:S(2)}) copy-start(f32[8,384,48]{1,2,0:T(8,128)} %param.12) | copy-start | bytes 1769476
  0.1 28.8 %copy-start.5 = (s32[512]{0:T(512)S(1)}, s32[512]{0:T(512)}, u32[]{:S(2)}) copy-start(s32[512]{0:T(512)} %param.16) | copy-start | bytes 6148
  0.1 28.9 %copy-start.1 = (bf16[512,192]{0,1:T(8,128)(2,1)S(1)}, bf16[512,192]{0,1:T(8,128)(2,1)}, u32[]{:S(2)}) copy-start(bf16[512,192]{0,1:T(8,128)(2,1)} %param.14) | copy-start | bytes 589828
  0.1 28.8 %copy-start.4 = (f32[512]{0:T(512)S(1)}, f32[512]{0:T(512)}, u32[]{:S(2)}) copy-start(f32[512]{0:T(512)} %param.15) | copy-start | bytes 6148
  0.1 44.5 %copy-start.6 = (s32[1,64]{1,0:T(1,128)S(1)}, s32[1,64]{1,0:T(1,128)}, u32[]{:S(2)}) copy-start(s32[1,64]{1,0:T(1,128)} %param.17) | copy-start | bytes 772
  25.8 36.0 %copy-start.3 = (f32[384]{0:T(512)S(1)}, f32[384]{0:T(512)}, u32[]{:S(2)}) copy-start(f32[384]{0:T(512)} %param.13) | copy-start | bytes 4612
  26.9 14.5 %collective-permute-start = (f32[384,384]{1,0:T(8,128)S(1)}, f32[384,384]{1,0:T(8,128)S(1)}, u32[]{:S(2)}, u32[]{:S(2)}) collective-permute-start(f32[384,384]{1,0:T(8,128)S(1)} %bitcast_select_fusion), channel_id=1, source_target_pairs={{0,4},{4,8},{8,12},{12,16},{16,20},{20,24},{24,28},{28,32},{32,36}... | collective-permute-start | bytes 1769480 | tf_op jit(solution)/shard_map/ppermute | solution.py:10
  42.7 30.2 %collective-permute-start.1 = (f32[384,384]{1,0:T(8,128)S(1)}, f32[384,384]{1,0:T(8,128)S(1)}, u32[]{:S(2)}, u32[]{:S(2)}) collective-permute-start(f32[384,384]{1,0:T(8,128)S(1)} %fusion.12), channel_id=1, source_target_pairs={{0,8},{4,12},{8,16},{12,20},{16,24},{20,28},{24,32},{28,36},{32,40... | collective-permute-start | bytes 1769480 | tf_op jit(solution)/shard_map/ppermute | solution.py:10
  47.8 24.3 %all-to-all-start = ((bf16[256,2,196]{2,1,0:T(2,128)(2,1)}), bf16[256,2,196]{2,1,0:T(2,128)(2,1)S(1)}, u32[]{:S(2)}, u32[]{:S(2)}) async-start(bf16[256,2,196]{2,1,0:T(2,128)(2,1)} %reshape.87), calls=%async_computation | async-start | bytes 524288 | tf_op jit(solution)/shard_map/all_to_all | solution.py:35
  74.2 22.8 %collective-permute-start.2 = (f32[384,384]{1,0:T(8,128)S(1)}, f32[384,384]{1,0:T(8,128)S(1)}, u32[]{:S(2)}, u32[]{:S(2)}) collective-permute-start(f32[384,384]{1,0:T(8,128)S(1)} %fusion.13), channel_id=1, source_target_pairs={{0,16},{4,20},{8,24},{12,28},{16,32},{20,36},{24,40},{28,44},{32,4... | collective-permute-start | bytes 1769480 | tf_op jit(solution)/shard_map/ppermute | solution.py:10
  98.2 42.0 %collective-permute-start.3 = (f32[384,384]{1,0:T(8,128)S(1)}, f32[384,384]{1,0:T(8,128)S(1)}, u32[]{:S(2)}, u32[]{:S(2)}) collective-permute-start(f32[384,384]{1,0:T(8,128)S(1)} %fusion.14), channel_id=1, source_target_pairs={{0,32},{4,36},{8,40},{12,44},{16,48},{20,52},{24,56},{28,60},{32,6... | collective-permute-start | bytes 1769480 | tf_op jit(solution)/shard_map/ppermute | solution.py:10
  132.0 8.2 %collective-permute-start.5 = (f32[384]{0:T(512)S(1)}, f32[384]{0:T(512)S(1)}, u32[]{:S(2)}, u32[]{:S(2)}) collective-permute-start(f32[384]{0:T(512)S(1)} %add_select_fusion), channel_id=1, source_target_pairs={{0,4},{4,8},{8,12},{12,16},{16,20},{20,24},{24,28},{28,32},{32,36}... | collective-permute-start | bytes 4616 | tf_op jit(solution)/shard_map/ppermute | solution.py:10
  141.5 65.4 %collective-permute-start.4 = (f32[384,384]{1,0:T(8,128)S(1)}, f32[384,384]{1,0:T(8,128)S(1)}, u32[]{:S(2)}, u32[]{:S(2)}) collective-permute-start(f32[384,384]{1,0:T(8,128)S(1)} %fusion.15), channel_id=1, source_target_pairs={{0,64},{4,68},{8,72},{12,76},{16,80},{20,84},{24,88},{28,92},{32,9... | collective-permute-start | bytes 1769480 | tf_op jit(solution)/shard_map/ppermute | solution.py:10
  145.1 26.3 %collective-permute-start.6 = (f32[384]{0:T(512)S(1)}, f32[384]{0:T(512)S(1)}, u32[]{:S(2)}, u32[]{:S(2)}) collective-permute-start(f32[384]{0:T(512)S(1)} %add.36), channel_id=1, source_target_pairs={{0,8},{4,12},{8,16},{12,20},{16,24},{20,28},{24,32},{28,36},{32,40... | collective-permute-start | bytes 4616 | tf_op jit(solution)/shard_map/ppermute | solution.py:10
  171.4 52.0 %copy-start.2 = (f32[8,384]{1,0:T(8,128)S(1)}, f32[8,384]{1,0:T(8,128)}, u32[]{:S(2)}) copy-start(f32[8,384]{1,0:T(8,128)} %get-tuple-element.55) | copy-start | bytes 36868
  172.1 9.1 %collective-permute-start.7 = (f32[384]{0:T(512)S(1)}, f32[384]{0:T(512)S(1)}, u32[]{:S(2)}, u32[]{:S(2)}) collective-permute-start(f32[384]{0:T(512)S(1)} %add.37), channel_id=1, source_target_pairs={{0,16},{4,20},{8,24},{12,28},{16,32},{20,36},{24,40},{28,44},{32,4... | collective-permute-start | bytes 4616 | tf_op jit(solution)/shard_map/ppermute | solution.py:10
  181.8 6.7 %collective-permute-start.8 = (f32[384]{0:T(512)S(1)}, f32[384]{0:T(512)S(1)}, u32[]{:S(2)}, u32[]{:S(2)}) collective-permute-start(f32[384]{0:T(512)S(1)} %add.38), channel_id=1, source_target_pairs={{0,32},{4,36},{8,40},{12,44},{16,48},{20,52},{24,56},{28,60},{32,6... | collective-permute-start | bytes 4616 | tf_op jit(solution)/shard_map/ppermute | solution.py:10
  189.2 7.6 %collective-permute-start.9 = (f32[384]{0:T(512)S(1)}, f32[384]{0:T(512)S(1)}, u32[]{:S(2)}, u32[]{:S(2)}) collective-permute-start(f32[384]{0:T(512)S(1)} %add.39), channel_id=1, source_target_pairs={{0,64},{4,68},{8,72},{12,76},{16,80},{20,84},{24,88},{28,92},{32,9... | collective-permute-start | bytes 4616 | tf_op jit(solution)/shard_map/ppermute | solution.py:10
  197.5 9.4 %collective-permute-start.10 = (f32[384]{0:T(512)S(1)}, f32[384]{0:T(512)S(1)}, u32[]{:S(2)}, u32[]{:S(2)}) collective-permute-start(f32[384]{0:T(512)S(1)} %add.40), channel_id=1, source_target_pairs={{0,128},{4,132},{8,136},{12,140},{16,144},{20,148},{24,152},{28,15... | collective-permute-start | bytes 4616 | tf_op jit(solution)/shard_map/ppermute | solution.py:10
  208.8 8.2 %collective-permute-start.11 = (f32[384]{0:T(512)S(1)}, f32[384]{0:T(512)S(1)}, u32[]{:S(2)}, u32[]{:S(2)}) collective-permute-start(f32[384]{0:T(512)S(1)} %add.41), channel_id=1, source_target_pairs={{0,4},{4,8},{8,12},{12,16},{16,20},{20,24},{24,28},{28,32},{32,36}... | collective-permute-start | bytes 4616 | tf_op jit(solution)/shard_map/ppermute | solution.py:10
where the time goes:
time: 226 us; the launch traced here: 224 us
  waiting for transfers between devices  83.5 us (37%)
  matrix products  59.6 us (26%)
  starting transfers between devices  39.5 us (17%)
  local copies, waits for them, and re-layouts  22.4 us (10%)
  blocking collectives  15.5 us (7%)
  other arithmetic  2.82 us (1%)
    ppermute x12, waiting for transfers between devices, passed_along(): return lax.ppermute(block, axis, route)  74.9 us
    ppermute x12, starting transfers between devices, passed_along(): return lax.ppermute(block, axis, route)  25.6 us
    dot_general x8, matrix products, compose(): prefix = jnp.dot(step_map, prefix, precision=exact)  25.3 us
    psum x1, blocking collectives, on_device(): forcing = lax.psum(partial_force, 'ingest')  15.5 us
    all_to_all x1, starting transfers between devices, on_device(): lax.all_to_all(sent, ('tm', 'ingest'), split_axis=0, concat_axis=0, tiled...  13.9 us
    dot_general x8, matrix products, advance(): offset = jnp.dot(step_map, offset, precision=exact) + step_force  13.8 us
    dynamic_update_slice x8, local copies, waits for them, and re-layouts, on_device(): lax.scan(advance, jnp.zeros((state_width,), jnp.float32), (trans, forcing))  10.6 us
    all_to_all x1, waiting for transfers between devices, on_device(): lax.all_to_all(sent, ('tm', 'ingest'), split_axis=0, concat_axis=0, tiled...  8.65 us
  transfers between devices with their start and end apart: 13, of which 9 were waited for; matrix products, arithmetic and copies ran while one was open for 20% of the time, Pallas kernels for 0%

commit v1 on v0

--- a/solution.py
+++ b/solution.py
@@ -39,7 +39,7 @@
     onehot = (got_marks[:, None] == step_ids).astype(jnp.bfloat16)
     drive_piece = jnp.einsum("rl,rq->lq", onehot, got_rows, preferred_element_type=jnp.float32)
     partial_force = jnp.einsum("lsq,lq->ls", gain, drive_piece, precision=exact)
-    forcing = lax.psum(partial_force, "ingest")
+    forcing = lax.all_gather(partial_force, "ingest").sum(axis=0)
 
     def compose(prefix, step_map):
         prefix = jnp.dot(step_map, prefix, precision=exact)

time: 226 us -> 216 us (0.956)
  waiting for transfers between devices: 83.5 us -> 76.6 us
  blocking collectives: 15.5 us -> 12 us
    psum x1 -> x0, blocking collectives: 15.5 us -> none  [on_device(): forcing = lax.psum(partial_force, 'ingest')]
    all_gather x0 -> x1, blocking collectives: none -> 12 us  [on_device(): forcing = lax.all_gather(partial_force, 'ingest').sum(axis=0)]
    all_to_all x1, waiting for transfers between devices: 8.65 us -> 4.14 us  [on_device(): lax.all_to_all(sent, ('tm', 'ingest'), split_axis=0, concat_axis=0, tiled...]
    ppermute x12, waiting for transfers between devices: 74.9 us -> 72.5 us  [passed_along(): return lax.ppermute(block, axis, route)]
  transfers between devices with their start and end apart: 13 -> 13, of which waited for: 9 -> 10; matrix products, arithmetic and copies ran while one was open for 20% -> 22% of each run, Pallas kernels for 0% -> 0%
where the time goes in v1:
time: 216 us; the launch traced here: 214 us
  waiting for transfers between devices  76.6 us (35%)
  matrix products  59.6 us (28%)
  starting transfers between devices  38.9 us (18%)
  local copies, waits for them, and re-layouts  22.4 us (10%)
  blocking collectives  12 us (6%)
  other arithmetic  3.42 us (2%)
    ppermute x12, waiting for transfers between devices, passed_along(): return lax.ppermute(block, axis, route)  72.5 us
    dot_general x8, matrix products, compose(): prefix = jnp.dot(step_map, prefix, precision=exact)  25.3 us
    ppermute x12, starting transfers between devices, passed_along(): return lax.ppermute(block, axis, route)  24.1 us
    all_to_all x1, starting transfers between devices, on_device(): lax.all_to_all(sent, ('tm', 'ingest'), split_axis=0, concat_axis=0, tiled...  14.8 us
    dot_general x8, matrix products, advance(): offset = jnp.dot(step_map, offset, precision=exact) + step_force  13.8 us
    all_gather x1, blocking collectives, on_device(): forcing = lax.all_gather(partial_force, 'ingest').sum(axis=0)  12 us
    dynamic_update_slice x8, local copies, waits for them, and re-layouts, on_device(): lax.scan(advance, jnp.zeros((state_width,), jnp.float32), (trans, forcing))  10.6 us
    dot_general x1, matrix products, on_device(): jnp.einsum('lsq,q->ls', prefix_maps, entering, precision=exact) + offsets  6.36 us
  transfers between devices with their start and end apart: 13, of which 10 were waited for; matrix products, arithmetic and copies ran while one was open for 22% of the time, Pallas kernels for 0%

profile of v1, /device:TPU:128, one launch (start us, length us, event | category | flops | bytes accessed | tf_op | source)
XLA Modules:
  0.0 213.7 jit_solution(13174679708959057509)
XLA Ops:
  0.1 25.7 %while.25 = (s32[]{:T(128)}, f32[384,384]{1,0:T(8,128)S(1)}, f32[8,384,384]{2,1,0:T(8,128)}, f32[8,384,384]{2,1,0:T(8,128)}, s32[]{:T(128)}) while((s32[]{:T(128)}, f32[384,384]{1,0:T(8,128)S(1)}, f32[8,384,384]{2,1,0:T(8,128)}, f32[8,384,384]{2,1,0:T(8,128)}, s32[]{:T(128)}) %tuple.41), condition=%wide.region_1.2_spmd, body=%wide.region_0.1_spmd.sunk | while | flops 679477248 | bytes 3540037 | solution.py:48
  0.2 3.2 %bitcast_dynamic-update-slice_fusion.2 = (f32[8,384,384]{2,1,0:T(8,128)}, f32[384,384]{1,0:T(8,128)S(1)}) fusion(f32[8,384,384]{2,1,0:T(8,128)} %get-tuple-element.182, s32[]{:T(128)S(6)} %copy.46, f32[384,384]{1,0:T(8,128)S(1)} %copy.53, f32[8,384,384]{2,1,0:T(8,128)} %get-tuple-element.188), kind=kOutput, calls=%fused_computation.clone.1 | convolution fusion | flops 679477248 | bytes 2360320 | tf_op jit(solution)/shard_map/while/body/eval_jaxpr/dot_general | solution.py:45
  3.4 3.1 %bitcast_dynamic-update-slice_fusion.2 = (f32[8,384,384]{2,1,0:T(8,128)}, f32[384,384]{1,0:T(8,128)S(1)}) fusion(f32[8,384,384]{2,1,0:T(8,128)} %get-tuple-element.182, s32[]{:T(128)S(6)} %copy.46, f32[384,384]{1,0:T(8,128)S(1)} %copy.53, f32[8,384,384]{2,1,0:T(8,128)} %get-tuple-element.188), kind=kOutput, calls=%fused_computation.clone.1 | convolution fusion | flops 679477248 | bytes 2360320 | tf_op jit(solution)/shard_map/while/body/eval_jaxpr/dot_general | solution.py:45
  6.6 3.2 %bitcast_dynamic-update-slice_fusion.2 = (f32[8,384,384]{2,1,0:T(8,128)}, f32[384,384]{1,0:T(8,128)S(1)}) fusion(f32[8,384,384]{2,1,0:T(8,128)} %get-tuple-element.182, s32[]{:T(128)S(6)} %copy.46, f32[384,384]{1,0:T(8,128)S(1)} %copy.53, f32[8,384,384]{2,1,0:T(8,128)} %get-tuple-element.188), kind=kOutput, calls=%fused_computation.clone.1 | convolution fusion | flops 679477248 | bytes 2360320 | tf_op jit(solution)/shard_map/while/body/eval_jaxpr/dot_general | solution.py:45
  9.8 3.2 %bitcast_dynamic-update-slice_fusion.2 = (f32[8,384,384]{2,1,0:T(8,128)}, f32[384,384]{1,0:T(8,128)S(1)}) fusion(f32[8,384,384]{2,1,0:T(8,128)} %get-tuple-element.182, s32[]{:T(128)S(6)} %copy.46, f32[384,384]{1,0:T(8,128)S(1)} %copy.53, f32[8,384,384]{2,1,0:T(8,128)} %get-tuple-element.188), kind=kOutput, calls=%fused_computation.clone.1 | convolution fusion | flops 679477248 | bytes 2360320 | tf_op jit(solution)/shard_map/while/body/eval_jaxpr/dot_general | solution.py:45
  13.0 3.2 %bitcast_dynamic-update-slice_fusion.2 = (f32[8,384,384]{2,1,0:T(8,128)}, f32[384,384]{1,0:T(8,128)S(1)}) fusion(f32[8,384,384]{2,1,0:T(8,128)} %get-tuple-element.182, s32[]{:T(128)S(6)} %copy.46, f32[384,384]{1,0:T(8,128)S(1)} %copy.53, f32[8,384,384]{2,1,0:T(8,128)} %get-tuple-element.188), kind=kOutput, calls=%fused_computation.clone.1 | convolution fusion | flops 679477248 | bytes 2360320 | tf_op jit(solution)/shard_map/while/body/eval_jaxpr/dot_general | solution.py:45
  16.2 3.1 %bitcast_dynamic-update-slice_fusion.2 = (f32[8,384,384]{2,1,0:T(8,128)}, f32[384,384]{1,0:T(8,128)S(1)}) fusion(f32[8,384,384]{2,1,0:T(8,128)} %get-tuple-element.182, s32[]{:T(128)S(6)} %copy.46, f32[384,384]{1,0:T(8,128)S(1)} %copy.53, f32[8,384,384]{2,1,0:T(8,128)} %get-tuple-element.188), kind=kOutput, calls=%fused_computation.clone.1 | convolution fusion | flops 679477248 | bytes 2360320 | tf_op jit(solution)/shard_map/while/body/eval_jaxpr/dot_general | solution.py:45
  19.4 3.1 %bitcast_dynamic-update-slice_fusion.2 = (f32[8,384,384]{2,1,0:T(8,128)}, f32[384,384]{1,0:T(8,128)S(1)}) fusion(f32[8,384,384]{2,1,0:T(8,128)} %get-tuple-element.182, s32[]{:T(128)S(6)} %copy.46, f32[384,384]{1,0:T(8,128)S(1)} %copy.53, f32[8,384,384]{2,1,0:T(8,128)} %get-tuple-element.188), kind=kOutput, calls=%fused_computation.clone.1 | convolution fusion | flops 679477248 | bytes 2360320 | tf_op jit(solution)/shard_map/while/body/eval_jaxpr/dot_general | solution.py:45
  22.6 3.1 %bitcast_dynamic-update-slice_fusion.2 = (f32[8,384,384]{2,1,0:T(8,128)}, f32[384,384]{1,0:T(8,128)S(1)}) fusion(f32[8,384,384]{2,1,0:T(8,128)} %get-tuple-element.182, s32[]{:T(128)S(6)} %copy.46, f32[384,384]{1,0:T(8,128)S(1)} %copy.53, f32[8,384,384]{2,1,0:T(8,128)} %get-tuple-element.188), kind=kOutput, calls=%fused_computation.clone.1 | convolution fusion | flops 679477248 | bytes 2360320 | tf_op jit(solution)/shard_map/while/body/eval_jaxpr/dot_general | solution.py:45
  26.9 1.9 collective-permute-start
  32.2 14.8 %all-to-all-start = ((bf16[256,2,196]{2,1,0:T(2,128)(2,1)}), bf16[256,2,196]{2,1,0:T(2,128)(2,1)S(1)}, u32[]{:S(2)}, u32[]{:S(2)}) async-start(bf16[256,2,196]{2,1,0:T(2,128)(2,1)} %reshape.88), calls=%async_computation | async-start | bytes 524288 | tf_op jit(solution)/shard_map/all_to_all | solution.py:35
  48.3 3.4 %collective-permute-start.1 = (f32[384,384]{1,0:T(8,128)S(1)}, f32[384,384]{1,0:T(8,128)S(1)}, u32[]{:S(2)}, u32[]{:S(2)}) collective-permute-start(f32[384,384]{1,0:T(8,128)S(1)} %fusion.12), channel_id=1, source_target_pairs={{0,8},{4,12},{8,16},{12,20},{16,24},{20,28},{24,32},{28,36},{32,40... | collective-permute-start | bytes 1769480 | tf_op jit(solution)/shard_map/ppermute | solution.py:10
  51.8 1.7 convolution_reduce_fusion.7
  53.5 4.1 %all-to-all-done = bf16[256,2,196]{2,1,0:T(2,128)(2,1)S(1)} async-done(((bf16[256,2,196]{2,1,0:T(2,128)(2,1)}), bf16[256,2,196]{2,1,0:T(2,128)(2,1)S(1)}, u32[]{:S(2)}, u32[]{:S(2)}) %all-to-all-start) | async-done | bytes 200736 | tf_op jit(solution)/shard_map/all_to_all | solution.py:35
  60.1 9.0 %collective-permute-done.1 = f32[384,384]{1,0:T(8,128)S(1)} collective-permute-done((f32[384,384]{1,0:T(8,128)S(1)}, f32[384,384]{1,0:T(8,128)S(1)}, u32[]{:S(2)}, u32[]{:S(2)}) %collective-permute-start.1) | collective-permute-done | bytes 589856 | tf_op jit(solution)/shard_map/ppermute | solution.py:10
  70.4 1.9 collective-permute-start.2
  72.3 1.7 fusion.7
  74.5 12.0 %all-gather = f32[32,384]{1,0:T(8,128)S(1)} all-gather(f32[8,384]{1,0:T(8,128)S(1)} %bitcast.76), channel_id=2, replica_groups=mesh['tm'=64,'ingest'=4] {'ingest'}, dimensions={0}, use_global_device_ids=true | all-gather | bytes 61440 | tf_op jit(solution)/shard_map/all_gather | solution.py:42
  87.2 3.2 %collective-permute-done.2 = f32[384,384]{1,0:T(8,128)S(1)} collective-permute-done((f32[384,384]{1,0:T(8,128)S(1)}, f32[384,384]{1,0:T(8,128)S(1)}, u32[]{:S(2)}, u32[]{:S(2)}) %collective-permute-start.2) | collective-permute-done | bytes 589856 | tf_op jit(solution)/shard_map/ppermute | solution.py:10
  91.6 1.9 collective-permute-start.3
  93.5 30.5 %while.26 = (s32[]{:T(128)}, f32[384]{0:T(512)S(1)}, f32[8,384]{1,0:T(8,128)}, f32[8,384,384]{2,1,0:T(8,128)}, f32[8,384]{1,0:T(8,128)}, /*index=5*/s32[]{:T(128)}, s32[]{:T(128)}) while((s32[]{:T(128)}, f32[384]{0:T(512)S(1)}, f32[8,384]{1,0:T(8,128)}, f32[8,384,384]{2,1,0:T(8,128)}, f32[8,384]{1,0:T(8,128)}, ...), condition=%wide.region_4.5_spmd.clone, body=%wide.region_3.4_spmd.clone.sunk | while | flops 1770243 | bytes 612971 | solution.py:55
  93.6 1.7 convolution_reduce_fusion.9
  96.0 1.3 dynamic_update_slice.13
  97.4 1.7 convolution_reduce_fusion.9
  101.2 1.7 convolution_reduce_fusion.9
  105.0 1.7 convolution_reduce_fusion.9
  108.8 1.7 convolution_reduce_fusion.9
  112.6 1.7 convolution_reduce_fusion.9
  115.1 1.3 dynamic_update_slice.13
  116.4 1.7 convolution_reduce_fusion.9
  118.9 1.3 dynamic_update_slice.13
  120.3 1.7 convolution_reduce_fusion.9
  122.7 1.3 dynamic_update_slice.13
  124.8 2.1 collective-permute-start.5
  126.9 6.1 %collective-permute-done.5 = f32[384]{0:T(512)S(1)} collective-permute-done((f32[384]{0:T(512)S(1)}, f32[384]{0:T(512)S(1)}, u32[]{:S(2)}, u32[]{:S(2)}) %collective-permute-start.5) | collective-permute-done | bytes 1568 | tf_op jit(solution)/shard_map/ppermute | solution.py:10
  134.3 1.9 collective-permute-start.4
  136.9 1.9 collective-permute-start.6
  138.8 22.2 %collective-permute-done.6 = f32[384]{0:T(512)S(1)} collective-permute-done((f32[384]{0:T(512)S(1)}, f32[384]{0:T(512)S(1)}, u32[]{:S(2)}, u32[]{:S(2)}) %collective-permute-start.6) | collective-permute-done | bytes 1568 | tf_op jit(solution)/shard_map/ppermute | solution.py:10
  161.7 1.9 collective-permute-start.7
  163.6 7.2 %collective-permute-done.7 = f32[384]{0:T(512)S(1)} collective-permute-done((f32[384]{0:T(512)S(1)}, f32[384]{0:T(512)S(1)}, u32[]{:S(2)}, u32[]{:S(2)}) %collective-permute-start.7) | collective-permute-done | bytes 1568 | tf_op jit(solution)/shard_map/ppermute | solution.py:10
  171.5 1.9 collective-permute-start.8
  173.4 4.8 %collective-permute-done.8 = f32[384]{0:T(512)S(1)} collective-permute-done((f32[384]{0:T(512)S(1)}, f32[384]{0:T(512)S(1)}, u32[]{:S(2)}, u32[]{:S(2)}) %collective-permute-start.8) | collective-permute-done | bytes 1568 | tf_op jit(solution)/shard_map/ppermute | solution.py:10
  178.8 1.9 collective-permute-start.9
  180.8 5.7 %collective-permute-done.9 = f32[384]{0:T(512)S(1)} collective-permute-done((f32[384]{0:T(512)S(1)}, f32[384]{0:T(512)S(1)}, u32[]{:S(2)}, u32[]{:S(2)}) %collective-permute-start.9) | collective-permute-done | bytes 1568 | tf_op jit(solution)/shard_map/ppermute | solution.py:10
  188.4 8.1 %collective-permute-done.10 = f32[384]{0:T(512)S(1)} collective-permute-done((f32[384]{0:T(512)S(1)}, f32[384]{0:T(512)S(1)}, u32[]{:S(2)}, u32[]{:S(2)}) %collective-permute-start.10) | collective-permute-done | bytes 1568 | tf_op jit(solution)/shard_map/ppermute | solution.py:10
  198.5 1.9 collective-permute-start.11
  200.4 6.3 %collective-permute-done.11 = f32[384]{0:T(512)S(1)} collective-permute-done((f32[384]{0:T(512)S(1)}, f32[384]{0:T(512)S(1)}, u32[]{:S(2)}, u32[]{:S(2)}) %collective-permute-start.11) | collective-permute-done | bytes 1568 | tf_op jit(solution)/shard_map/ppermute | solution.py:10
  206.7 6.4 %fusion.18 = f32[1,8,384]{2,0,1:T(1,128)S(1)} fusion(f32[8,384,384]{2,1,0:T(8,128)} %get-tuple-element.54, f32[384,1,1]{0,1,2:T(1,128)S(1)} %reshape.76), kind=kOutput, calls=%fused_computation.43 | convolution fusion | flops 14155776 | bytes 4732416 | tf_op jit(solution)/shard_map/lsq,q->ls/dot_general | solution.py:74
  (127 shorter events, 32.6 us)
Async XLA Ops:
  0.0 74.1 %copy-start = (f32[8,384,48]{1,2,0:T(8,128)S(1)}, f32[8,384,48]{1,2,0:T(8,128)}, u32[]{:S(2)}) copy-start(f32[8,384,48]{1,2,0:T(8,128)} %param.12) | copy-start | bytes 1769476
  0.1 28.8 %copy-start.5 = (s32[512]{0:T(512)S(1)}, s32[512]{0:T(512)}, u32[]{:S(2)}) copy-start(s32[512]{0:T(512)} %param.16) | copy-start | bytes 6148
  0.1 28.9 %copy-start.1 = (bf16[512,192]{0,1:T(8,128)(2,1)S(1)}, bf16[512,192]{0,1:T(8,128)(2,1)}, u32[]{:S(2)}) copy-start(bf16[512,192]{0,1:T(8,128)(2,1)} %param.14) | copy-start | bytes 589828
  0.1 28.8 %copy-start.4 = (f32[512]{0:T(512)S(1)}, f32[512]{0:T(512)}, u32[]{:S(2)}) copy-start(f32[512]{0:T(512)} %param.15) | copy-start | bytes 6148
  0.1 29.8 %copy-start.6 = (s32[1,64]{1,0:T(1,128)S(1)}, s32[1,64]{1,0:T(1,128)}, u32[]{:S(2)}) copy-start(s32[1,64]{1,0:T(1,128)} %param.17) | copy-start | bytes 772
  25.8 26.0 %copy-start.3 = (f32[384]{0:T(512)S(1)}, f32[384]{0:T(512)}, u32[]{:S(2)}) copy-start(f32[384]{0:T(512)} %param.13) | copy-start | bytes 4612
  26.9 20.2 %collective-permute-start = (f32[384,384]{1,0:T(8,128)S(1)}, f32[384,384]{1,0:T(8,128)S(1)}, u32[]{:S(2)}, u32[]{:S(2)}) collective-permute-start(f32[384,384]{1,0:T(8,128)S(1)} %bitcast_select_fusion), channel_id=1, source_target_pairs={{0,4},{4,8},{8,12},{12,16},{16,20},{20,24},{24,28},{28,32},{32,36}... | collective-permute-start | bytes 1769480 | tf_op jit(solution)/shard_map/ppermute | solution.py:10
  32.2 25.5 %all-to-all-start = ((bf16[256,2,196]{2,1,0:T(2,128)(2,1)}), bf16[256,2,196]{2,1,0:T(2,128)(2,1)S(1)}, u32[]{:S(2)}, u32[]{:S(2)}) async-start(bf16[256,2,196]{2,1,0:T(2,128)(2,1)} %reshape.88), calls=%async_computation | async-start | bytes 524288 | tf_op jit(solution)/shard_map/all_to_all | solution.py:35
  48.3 20.8 %collective-permute-start.1 = (f32[384,384]{1,0:T(8,128)S(1)}, f32[384,384]{1,0:T(8,128)S(1)}, u32[]{:S(2)}, u32[]{:S(2)}) collective-permute-start(f32[384,384]{1,0:T(8,128)S(1)} %fusion.12), channel_id=1, source_target_pairs={{0,8},{4,12},{8,16},{12,20},{16,24},{20,28},{24,32},{28,36},{32,40... | collective-permute-start | bytes 1769480 | tf_op jit(solution)/shard_map/ppermute | solution.py:10
  70.4 19.9 %collective-permute-start.2 = (f32[384,384]{1,0:T(8,128)S(1)}, f32[384,384]{1,0:T(8,128)S(1)}, u32[]{:S(2)}, u32[]{:S(2)}) collective-permute-start(f32[384,384]{1,0:T(8,128)S(1)} %fusion.13), channel_id=1, source_target_pairs={{0,16},{4,20},{8,24},{12,28},{16,32},{20,36},{24,40},{28,44},{32,4... | collective-permute-start | bytes 1769480 | tf_op jit(solution)/shard_map/ppermute | solution.py:10
  91.6 41.4 %collective-permute-start.3 = (f32[384,384]{1,0:T(8,128)S(1)}, f32[384,384]{1,0:T(8,128)S(1)}, u32[]{:S(2)}, u32[]{:S(2)}) collective-permute-start(f32[384,384]{1,0:T(8,128)S(1)} %fusion.14), channel_id=1, source_target_pairs={{0,32},{4,36},{8,40},{12,44},{16,48},{20,52},{24,56},{28,60},{32,6... | collective-permute-start | bytes 1769480 | tf_op jit(solution)/shard_map/ppermute | solution.py:10
  124.8 8.2 %collective-permute-start.5 = (f32[384]{0:T(512)S(1)}, f32[384]{0:T(512)S(1)}, u32[]{:S(2)}, u32[]{:S(2)}) collective-permute-start(f32[384]{0:T(512)S(1)} %add_select_fusion), channel_id=1, source_target_pairs={{0,4},{4,8},{8,12},{12,16},{16,20},{20,24},{24,28},{28,32},{32,36}... | collective-permute-start | bytes 4616 | tf_op jit(solution)/shard_map/ppermute | solution.py:10
  134.3 62.2 %collective-permute-start.4 = (f32[384,384]{1,0:T(8,128)S(1)}, f32[384,384]{1,0:T(8,128)S(1)}, u32[]{:S(2)}, u32[]{:S(2)}) collective-permute-start(f32[384,384]{1,0:T(8,128)S(1)} %fusion.15), channel_id=1, source_target_pairs={{0,64},{4,68},{8,72},{12,76},{16,80},{20,84},{24,88},{28,92},{32,9... | collective-permute-start | bytes 1769480 | tf_op jit(solution)/shard_map/ppermute | solution.py:10
  136.9 24.1 %collective-permute-start.6 = (f32[384]{0:T(512)S(1)}, f32[384]{0:T(512)S(1)}, u32[]{:S(2)}, u32[]{:S(2)}) collective-permute-start(f32[384]{0:T(512)S(1)} %add.34), channel_id=1, source_target_pairs={{0,8},{4,12},{8,16},{12,20},{16,24},{20,28},{24,32},{28,36},{32,40... | collective-permute-start | bytes 4616 | tf_op jit(solution)/shard_map/ppermute | solution.py:10
  161.0 52.0 %copy-start.2 = (f32[8,384]{1,0:T(8,128)S(1)}, f32[8,384]{1,0:T(8,128)}, u32[]{:S(2)}) copy-start(f32[8,384]{1,0:T(8,128)} %get-tuple-element.55) | copy-start | bytes 36868
  161.7 9.1 %collective-permute-start.7 = (f32[384]{0:T(512)S(1)}, f32[384]{0:T(512)S(1)}, u32[]{:S(2)}, u32[]{:S(2)}) collective-permute-start(f32[384]{0:T(512)S(1)} %add.35), channel_id=1, source_target_pairs={{0,16},{4,20},{8,24},{12,28},{16,32},{20,36},{24,40},{28,44},{32,4... | collective-permute-start | bytes 4616 | tf_op jit(solution)/shard_map/ppermute | solution.py:10
  171.5 6.7 %collective-permute-start.8 = (f32[384]{0:T(512)S(1)}, f32[384]{0:T(512)S(1)}, u32[]{:S(2)}, u32[]{:S(2)}) collective-permute-start(f32[384]{0:T(512)S(1)} %add.36), channel_id=1, source_target_pairs={{0,32},{4,36},{8,40},{12,44},{16,48},{20,52},{24,56},{28,60},{32,6... | collective-permute-start | bytes 4616 | tf_op jit(solution)/shard_map/ppermute | solution.py:10
  178.8 7.6 %collective-permute-start.9 = (f32[384]{0:T(512)S(1)}, f32[384]{0:T(512)S(1)}, u32[]{:S(2)}, u32[]{:S(2)}) collective-permute-start(f32[384]{0:T(512)S(1)} %add.37), channel_id=1, source_target_pairs={{0,64},{4,68},{8,72},{12,76},{16,80},{20,84},{24,88},{28,92},{32,9... | collective-permute-start | bytes 4616 | tf_op jit(solution)/shard_map/ppermute | solution.py:10
  187.1 9.4 %collective-permute-start.10 = (f32[384]{0:T(512)S(1)}, f32[384]{0:T(512)S(1)}, u32[]{:S(2)}, u32[]{:S(2)}) collective-permute-start(f32[384]{0:T(512)S(1)} %add.38), channel_id=1, source_target_pairs={{0,128},{4,132},{8,136},{12,140},{16,144},{20,148},{24,152},{28,15... | collective-permute-start | bytes 4616 | tf_op jit(solution)/shard_map/ppermute | solution.py:10
  198.5 8.2 %collective-permute-start.11 = (f32[384]{0:T(512)S(1)}, f32[384]{0:T(512)S(1)}, u32[]{:S(2)}, u32[]{:S(2)}) collective-permute-start(f32[384]{0:T(512)S(1)} %add.39), channel_id=1, source_target_pairs={{0,4},{4,8},{8,12},{12,16},{16,20},{20,24},{24,28},{28,32},{32,36}... | collective-permute-start | bytes 4616 | tf_op jit(solution)/shard_map/ppermute | solution.py:10
